TPU v7x, 32 devices: a whole 2x2x4 slice. The times are simulated.
32 devices in a mesh: row: 8 (over y, x, core), col: 4 (over z).
Axes of the slice: x: 2, y: 2, z: 4, core: 2. Of those that a mesh axis runs over, the one named last changes fastest.
Arguments:
- adjacency: float32 [1024, 32768], P('row', 'col'), may hold values from 0 to 0.99, as said below
Outputs:
- tom: float32 [1024, 1024], P('row', 'col')
Inputs may be any that keep to these rules, and one draw needn't show every extreme that they name: `adjacency`: every entry is nonnegative and below 0.99.
All inputs are finite; a program needn't handle non-finite values.
Results may differ from a plain program's by a relative error of at most 0.000059.
Values sent between devices are 32-bit elements; how exact they have to be, the bound alone decides.
No kernel may reach another device: no remote copies, remote signals or barrier semaphores. Data moves between devices by JAX's collectives and lax.ppermute only.
A program may use at most 64 MiB of HBM per device.

v0:
```python
import jax
import jax.numpy as jnp
from jax import lax
from jax.sharding import PartitionSpec as P


def inner_rows(left, right):
    return lax.dot_general(
        left,
        right,
        (((1,), (1,)), ((), ())),
        precision=lax.Precision.HIGHEST,
        preferred_element_type=jnp.float32,
    )


def body(adjacency):
    strip_rows = adjacency.shape[0]
    window = strip_rows * lax.axis_size("row") // lax.axis_size("col")
    pieces = lax.all_to_all(adjacency, "row", split_axis=1, concat_axis=0, tiled=True)
    block_sums = lax.psum_scatter(
        inner_rows(pieces, pieces), "col", scatter_dimension=0, tiled=True
    )
    shared_sum = lax.psum_scatter(block_sums, "row", scatter_dimension=1, tiled=True).T
    own_degree = lax.psum(jnp.sum(adjacency, axis=1), "col")
    all_degree = lax.all_gather(own_degree, "row", axis=0, tiled=True)
    col_degree = lax.dynamic_slice_in_dim(all_degree, lax.axis_index("col") * window, window, 0)
    linked = adjacency[:, :window]
    smaller = jnp.minimum(own_degree[:, None], col_degree[None, :])
    return (shared_sum + linked) / (smaller + 1.0 - linked)


def solution(mesh):
    placed = (P("row", "col"),)
    return jax.shard_map(
        body, mesh=mesh, in_specs=placed, out_specs=P("row", "col"), check_vma=False
    )
```

profile of v0, /device:TPU:0, one launch (start us, length us, event | category | flops | bytes accessed | tf_op | source)
XLA Modules:
  0.0 215.7 jit_solution(15998971876274687652)
XLA Ops:
  6.5 0.0 reduce-scatter.3.cloned.1.call-start
  6.5 5.6 %copy.10 = f32[128,8192]{0,1:T(8,128)} copy(f32[128,8192]{1,0:T(8,128)} %param.1) | data formatting | bytes 8388608 | tf_op args[0]
  12.1 54.3 %all_to_all.19 = f32[128,8,1024]{0,2,1:T(8,128)} all-to-all(f32[128,8,1024]{0,2,1:T(8,128)} %bitcast.11), channel_id=1, replica_groups=mesh['row'=8,'col'=4] {'row'}, dimensions={1} | all-to-all | bytes 8388608 | tf_op jit(solution)/shard_map/all_to_all | solution.py:20
  66.4 5.3 %copy.11 = f32[8,128,1024]{2,1,0:T(8,128)} copy(f32[8,128,1024]{1,2,0:T(8,128)} %bitcast.12) | data formatting | bytes 8388608 | tf_op jit(solution)/shard_map/all_to_all | solution.py:20
  71.8 18.1 %fusion.1 = f32[1024,1024]{1,0:T(8,128)} fusion(f32[1024,1024]{1,0:T(8,128)} %bitcast.13), kind=kOutput, calls=%fused_computation.2 | convolution fusion | flops 12884901888 | bytes 8388608 | tf_op jit(solution)/shard_map/dot_general | solution.py:8
  89.9 0.0 reduce-scatter.3.cloned.1.call-update
  89.9 0.0 reduce-scatter.5.cloned.1.call-start
  90.0 76.9 %reduce-scatter.3.cloned.1.call-done = f32[256,1024]{1,0:T(8,128)} async-done(((f32[1024,1024]{1,0:T(8,128)}), f32[256,1024]{1,0:T(8,128)}) %reduce-scatter.3.cloned.1.call-update) | async-done | bytes 1048592 | tf_op jit(solution)/shard_map/reduce_scatter | solution.py:21
  166.9 0.0 reduce-scatter.5.cloned.1.call-update
  166.9 2.5 %reduce_sum.9 = f32[128]{0:T(128)S(1)} reduce(f32[128,8192]{1,0:T(8,128)} %param.1, f32[]{:T(128)} %constant.6.clone.1), dimensions={1}, to_apply=%region_2.0 | reduce | flops 1048448 | bytes 4194820 | tf_op jit(solution)/shard_map/reduce_sum | solution.py:25
  169.4 11.0 %psum.7 = f32[128]{0:T(128)S(1)} all-reduce(f32[128]{0:T(128)S(1)} %reduce_sum.9), channel_id=1, replica_groups=mesh['row'=8,'col'=4] {'col'}, use_global_device_ids=true, to_apply=%region_3.0 | all-reduce | flops 128 | bytes 1024 | tf_op jit(solution)/shard_map/psum | solution.py:25
  180.4 8.9 %all-gather = f32[8,1,128]{2,1,0:T(1,128)S(1)} all-gather(f32[1,1,128]{2,1,0:T(1,128)S(1)} %bitcast.15), channel_id=1, replica_groups=mesh['row'=8,'col'=4] {'row'}, dimensions={0}, use_global_device_ids=true | all-gather | bytes 4608 | tf_op jit(solution)/shard_map/all_gather | solution.py:26
  189.3 0.1 dynamic_slice.3
  189.4 17.6 %reduce-scatter.5.cloned.1.call-done = f32[256,128]{1,0:T(8,128)} async-done(((f32[256,1024]{1,0:T(8,128)}), f32[256,128]{1,0:T(8,128)}) %reduce-scatter.5.cloned.1.call-update) | async-done | bytes 131088 | tf_op jit(solution)/shard_map/reduce_scatter | solution.py:24
  207.0 1.1 fusion
  208.1 0.8 copy.13
Async XLA Ops:
  6.5 160.4 %reduce-scatter.3.cloned.1.call-start = ((), (), s32[]{:S(2)}) async-start(), calls=%async_computation.3 | async-start | bytes 5242880 | tf_op jit(solution)/shard_map/reduce_scatter | solution.py:21
  89.9 117.1 %reduce-scatter.5.cloned.1.call-start = ((), (), s32[]{:S(2)}) async-start(), calls=%async_computation.4 | async-start | bytes 1179648 | tf_op jit(solution)/shard_map/reduce_scatter | solution.py:24
Sparse Core Ops, SparseCore 0:
  90.1 76.8 reduce-scatter.2
  170.4 36.5 reduce-scatter.4
where the time goes:
time: 216 us
  waiting for transfers between devices  94.6 us (44%)
  blocking collectives  74.2 us (34%)
  matrix products  18.1 us (8%)
  between operations  13.4 us (6%)
  local copies, waits for them, and re-layouts  11.7 us (5%)
  other arithmetic  3.57 us (2%)
    reduce_scatter x1, waiting for transfers between devices, body(): lax.psum_scatter(inner_rows(pieces, pieces), 'col', scatter_dimension=0,...  76.9 us
    all_to_all x1, blocking collectives, body(): lax.all_to_all(adjacency, 'row', split_axis=1, concat_axis=0, tiled=True)  54.3 us
    dot_general x1, matrix products, inner_rows(): lax.dot_general(left, right, (((1,), (1,)), ((), ())), precision=lax.Prec...  18.1 us
    reduce_scatter x1, waiting for transfers between devices, body(): lax.psum_scatter(block_sums, 'row', scatter_dimension=1, tiled=True)  17.6 us
    psum x1, blocking collectives, body(): own_degree = lax.psum(jnp.sum(adjacency, axis=1), 'col')  11 us
    all_gather x1, blocking collectives, body(): all_degree = lax.all_gather(own_degree, 'row', axis=0, tiled=True)  8.92 us
    unnamed x1, local copies, waits for them, and re-layouts  5.57 us
    all_to_all x1, local copies, waits for them, and re-layouts, body(): lax.all_to_all(adjacency, 'row', split_axis=1, concat_axis=0, tiled=True)  5.34 us
  transfers between devices with their start and end apart: 2, of which 2 were waited for; matrix products, arithmetic and copies ran while one was open for 1% of the time, Pallas kernels for 0%

commit v1 on v0

--- a/solution.py
+++ b/solution.py
@@ -2,6 +2,16 @@
 import jax.numpy as jnp
 from jax import lax
 from jax.sharding import PartitionSpec as P
+
+
+def pass_along(x, axis, dim):
+    n_dev = lax.axis_size(axis)
+    held, tiles = (x, [x])
+    for _ in range(n_dev - 1):
+        held = lax.ppermute(held, axis, [(i, (i + 1) % n_dev) for i in range(n_dev)])
+        tiles.insert(0, held)
+    flat = jnp.concatenate(tiles, axis=dim)
+    return jnp.roll(flat, (lax.axis_index(axis) + 1) * x.shape[dim], axis=dim)
 
 
 def inner_rows(left, right):
@@ -23,7 +33,7 @@
     )
     shared_sum = lax.psum_scatter(block_sums, "row", scatter_dimension=1, tiled=True).T
     own_degree = lax.psum(jnp.sum(adjacency, axis=1), "col")
-    all_degree = lax.all_gather(own_degree, "row", axis=0, tiled=True)
+    all_degree = pass_along(own_degree, "row", 0)
     col_degree = lax.dynamic_slice_in_dim(all_degree, lax.axis_index("col") * window, window, 0)
     linked = adjacency[:, :window]
     smaller = jnp.minimum(own_degree[:, None], col_degree[None, :])

time: 216 us -> 216 us (level)
  blocking collectives: 74.2 us -> 67.3 us
  waiting for transfers between devices: 94.6 us -> 101 us
    reduce_scatter x1, waiting for transfers between devices: 76.9 us -> 34.6 us  [body(): lax.psum_scatter(inner_rows(pieces, pieces), 'col', scatter_dimension=0,...]
    ppermute x0 -> x7, waiting for transfers between devices: none -> 27 us  [pass_along(): lax.ppermute(held, axis, [(i, (i + 1) % n_dev) for i in range(n_dev)])]
    reduce_scatter x1, waiting for transfers between devices: 17.6 us -> 39.6 us  [body(): lax.psum_scatter(block_sums, 'row', scatter_dimension=1, tiled=True)]
    all_gather x1 -> x0, blocking collectives: 8.92 us -> none  [body(): all_degree = lax.all_gather(own_degree, 'row', axis=0, tiled=True)]
    unnamed x1 -> x16, local copies, waits for them, and re-layouts: 5.57 us -> 5.66 us
  transfers between devices with their start and end apart: 2 -> 9, of which waited for: 2 -> 9; matrix products, arithmetic and copies ran while one was open for 1% -> 1% of each run, Pallas kernels for 0% -> 0%
where the time goes in v1:
time: 216 us
  waiting for transfers between devices  101 us (47%)
  blocking collectives  67.3 us (31%)
  matrix products  18.1 us (8%)
  between operations  13.5 us (6%)
  local copies, waits for them, and re-layouts  11.9 us (6%)
  other arithmetic  3.57 us (2%)
    all_to_all x1, blocking collectives, body(): lax.all_to_all(adjacency, 'row', split_axis=1, concat_axis=0, tiled=True)  54.3 us
    reduce_scatter x1, waiting for transfers between devices, body(): lax.psum_scatter(block_sums, 'row', scatter_dimension=1, tiled=True)  39.6 us
    reduce_scatter x1, waiting for transfers between devices, body(): lax.psum_scatter(inner_rows(pieces, pieces), 'col', scatter_dimension=0,...  34.6 us
    ppermute x7, waiting for transfers between devices, pass_along(): lax.ppermute(held, axis, [(i, (i + 1) % n_dev) for i in range(n_dev)])  27 us
    dot_general x1, matrix products, inner_rows(): lax.dot_general(left, right, (((1,), (1,)), ((), ())), precision=lax.Prec...  18.1 us
    psum x1, blocking collectives, body(): own_degree = lax.psum(jnp.sum(adjacency, axis=1), 'col')  13 us
    unnamed x16, local copies, waits for them, and re-layouts  5.66 us
    all_to_all x1, local copies, waits for them, and re-layouts, body(): lax.all_to_all(adjacency, 'row', split_axis=1, concat_axis=0, tiled=True)  5.35 us
  transfers between devices with their start and end apart: 9, of which 9 were waited for; matrix products, arithmetic and copies ran while one was open for 1% of the time, Pallas kernels for 0%

profile of v1, /device:TPU:0, one launch (start us, length us, event | category | flops | bytes accessed | tf_op | source)
XLA Modules:
  0.0 215.8 jit_solution(13704399934065595680)
XLA Ops:
  6.5 0.0 reduce-scatter.3.cloned.1.call-start
  6.5 5.6 %copy.6 = f32[128,8192]{0,1:T(8,128)} copy(f32[128,8192]{1,0:T(8,128)} %param.1) | data formatting | bytes 8388608 | tf_op args[0]
  12.1 54.3 %all_to_all.19 = f32[128,8,1024]{0,2,1:T(8,128)} all-to-all(f32[128,8,1024]{0,2,1:T(8,128)} %bitcast.9), channel_id=1, replica_groups=mesh['row'=8,'col'=4] {'row'}, dimensions={1} | all-to-all | bytes 8388608 | tf_op jit(solution)/shard_map/all_to_all | solution.py:30
  66.4 5.4 %copy.7 = f32[8,128,1024]{2,1,0:T(8,128)} copy(f32[8,128,1024]{1,2,0:T(8,128)} %bitcast.10) | data formatting | bytes 8388608 | tf_op jit(solution)/shard_map/all_to_all | solution.py:30
  71.8 18.1 %fusion.1 = f32[1024,1024]{1,0:T(8,128)} fusion(f32[1024,1024]{1,0:T(8,128)} %bitcast.11), kind=kOutput, calls=%fused_computation.18 | convolution fusion | flops 12884901888 | bytes 8388608 | tf_op jit(solution)/shard_map/dot_general | solution.py:18
  89.9 0.0 reduce-scatter.3.cloned.1.call-update
  90.0 0.0 reduce-scatter.5.cloned.1.call-start
  90.0 2.5 %reduce_sum.9 = f32[128]{0:T(128)S(1)} reduce(f32[128,8192]{1,0:T(8,128)} %param.1, f32[]{:T(128)} %constant.35.clone.1), dimensions={1}, to_apply=%region_2.0 | reduce | flops 1048448 | bytes 4194820 | tf_op jit(solution)/shard_map/reduce_sum | solution.py:35
  92.5 13.0 %psum.7 = f32[128]{0:T(128)S(1)} all-reduce(f32[128]{0:T(128)S(1)} %reduce_sum.9), channel_id=1, replica_groups=mesh['row'=8,'col'=4] {'col'}, use_global_device_ids=true, to_apply=%region_3.0 | all-reduce | flops 128 | bytes 1024 | tf_op jit(solution)/shard_map/psum | solution.py:35
  105.5 0.0 collective-permute-start
  105.6 3.9 %collective-permute-done = f32[128]{0:T(128)S(1)} collective-permute-done((f32[128]{0:T(128)S(1)}, f32[128]{0:T(128)S(1)}, u32[]{:S(2)}, u32[]{:S(2)}) %collective-permute-start) | collective-permute-done | bytes 544 | tf_op jit(solution)/shard_map/ppermute | solution.py:11
  109.4 0.0 collective-permute-start.1
  109.4 3.9 %collective-permute-done.1 = f32[128]{0:T(128)S(1)} collective-permute-done((f32[128]{0:T(128)S(1)}, f32[128]{0:T(128)S(1)}, u32[]{:S(2)}, u32[]{:S(2)}) %collective-permute-start.1) | collective-permute-done | bytes 544 | tf_op jit(solution)/shard_map/ppermute | solution.py:11
  113.3 0.0 collective-permute-start.2
  113.3 3.9 %collective-permute-done.2 = f32[128]{0:T(128)S(1)} collective-permute-done((f32[128]{0:T(128)S(1)}, f32[128]{0:T(128)S(1)}, u32[]{:S(2)}, u32[]{:S(2)}) %collective-permute-start.2) | collective-permute-done | bytes 544 | tf_op jit(solution)/shard_map/ppermute | solution.py:11
  117.1 0.0 collective-permute-start.3
  117.1 3.9 %collective-permute-done.3 = f32[128]{0:T(128)S(1)} collective-permute-done((f32[128]{0:T(128)S(1)}, f32[128]{0:T(128)S(1)}, u32[]{:S(2)}, u32[]{:S(2)}) %collective-permute-start.3) | collective-permute-done | bytes 544 | tf_op jit(solution)/shard_map/ppermute | solution.py:11
  121.0 0.0 collective-permute-start.4
  121.0 3.9 %collective-permute-done.4 = f32[128]{0:T(128)S(1)} collective-permute-done((f32[128]{0:T(128)S(1)}, f32[128]{0:T(128)S(1)}, u32[]{:S(2)}, u32[]{:S(2)}) %collective-permute-start.4) | collective-permute-done | bytes 544 | tf_op jit(solution)/shard_map/ppermute | solution.py:11
  124.9 0.0 collective-permute-start.5
  124.9 3.9 %collective-permute-done.5 = f32[128]{0:T(128)S(1)} collective-permute-done((f32[128]{0:T(128)S(1)}, f32[128]{0:T(128)S(1)}, u32[]{:S(2)}, u32[]{:S(2)}) %collective-permute-start.5) | collective-permute-done | bytes 544 | tf_op jit(solution)/shard_map/ppermute | solution.py:11
  128.7 0.0 collective-permute-start.6
  128.7 3.9 %collective-permute-done.6 = f32[128]{0:T(128)S(1)} collective-permute-done((f32[128]{0:T(128)S(1)}, f32[128]{0:T(128)S(1)}, u32[]{:S(2)}, u32[]{:S(2)}) %collective-permute-start.6) | collective-permute-done | bytes 544 | tf_op jit(solution)/shard_map/ppermute | solution.py:11
  132.6 34.6 %reduce-scatter.3.cloned.1.call-done = f32[256,1024]{1,0:T(8,128)} async-done(((f32[1024,1024]{1,0:T(8,128)}), f32[256,1024]{1,0:T(8,128)}) %reduce-scatter.3.cloned.1.call-update) | async-done | bytes 1048592 | tf_op jit(solution)/shard_map/reduce_scatter | solution.py:31
  167.2 0.0 reduce-scatter.5.cloned.1.call-update
  167.4 0.1 dynamic_slice.8
  167.5 39.6 %reduce-scatter.5.cloned.1.call-done = f32[256,128]{1,0:T(8,128)} async-done(((f32[256,1024]{1,0:T(8,128)}), f32[256,128]{1,0:T(8,128)}) %reduce-scatter.5.cloned.1.call-update) | async-done | bytes 131088 | tf_op jit(solution)/shard_map/reduce_scatter | solution.py:34
  207.1 1.1 fusion
  208.2 0.8 copy.9
  (17 shorter events, 0.1 us)
Async XLA Ops:
  6.5 160.6 %reduce-scatter.3.cloned.1.call-start = ((), (), s32[]{:S(2)}) async-start(), calls=%async_computation.3 | async-start | bytes 5242880 | tf_op jit(solution)/shard_map/reduce_scatter | solution.py:31
  90.0 117.2 %reduce-scatter.5.cloned.1.call-start = ((), (), s32[]{:S(2)}) async-start(), calls=%async_computation.4 | async-start | bytes 1179648 | tf_op jit(solution)/shard_map/reduce_scatter | solution.py:34
  105.5 3.9 %collective-permute-start = (f32[128]{0:T(128)S(1)}, f32[128]{0:T(128)S(1)}, u32[]{:S(2)}, u32[]{:S(2)}) collective-permute-start(f32[128]{0:T(128)S(1)} %psum.7), channel_id=1, source_target_pairs={{0,4},{4,8},{8,12},{12,16},{16,20},{20,24},{24,28},{28,0},{1,5},{5... | collective-permute-start | bytes 1544 | tf_op jit(solution)/shard_map/ppermute | solution.py:11
  109.4 3.9 %collective-permute-start.1 = (f32[128]{0:T(128)S(1)}, f32[128]{0:T(128)S(1)}, u32[]{:S(2)}, u32[]{:S(2)}) collective-permute-start(f32[128]{0:T(128)S(1)} %collective-permute-done), channel_id=1, source_target_pairs={{0,4},{4,8},{8,12},{12,16},{16,20},{20,24},{24,28},{28,0},{1,5},{5... | collective-permute-start | bytes 1544 | tf_op jit(solution)/shard_map/ppermute | solution.py:11
  113.3 3.9 %collective-permute-start.2 = (f32[128]{0:T(128)S(1)}, f32[128]{0:T(128)S(1)}, u32[]{:S(2)}, u32[]{:S(2)}) collective-permute-start(f32[128]{0:T(128)S(1)} %collective-permute-done.1), channel_id=1, source_target_pairs={{0,4},{4,8},{8,12},{12,16},{16,20},{20,24},{24,28},{28,0},{1,5},{5... | collective-permute-start | bytes 1544 | tf_op jit(solution)/shard_map/ppermute | solution.py:11
  117.1 3.9 %collective-permute-start.3 = (f32[128]{0:T(128)S(1)}, f32[128]{0:T(128)S(1)}, u32[]{:S(2)}, u32[]{:S(2)}) collective-permute-start(f32[128]{0:T(128)S(1)} %collective-permute-done.2), channel_id=1, source_target_pairs={{0,4},{4,8},{8,12},{12,16},{16,20},{20,24},{24,28},{28,0},{1,5},{5... | collective-permute-start | bytes 1544 | tf_op jit(solution)/shard_map/ppermute | solution.py:11
  121.0 3.9 %collective-permute-start.4 = (f32[128]{0:T(128)S(1)}, f32[128]{0:T(128)S(1)}, u32[]{:S(2)}, u32[]{:S(2)}) collective-permute-start(f32[128]{0:T(128)S(1)} %collective-permute-done.3), channel_id=1, source_target_pairs={{0,4},{4,8},{8,12},{12,16},{16,20},{20,24},{24,28},{28,0},{1,5},{5... | collective-permute-start | bytes 1544 | tf_op jit(solution)/shard_map/ppermute | solution.py:11
  124.9 3.9 %collective-permute-start.5 = (f32[128]{0:T(128)S(1)}, f32[128]{0:T(128)S(1)}, u32[]{:S(2)}, u32[]{:S(2)}) collective-permute-start(f32[128]{0:T(128)S(1)} %collective-permute-done.4), channel_id=1, source_target_pairs={{0,4},{4,8},{8,12},{12,16},{16,20},{20,24},{24,28},{28,0},{1,5},{5... | collective-permute-start | bytes 1544 | tf_op jit(solution)/shard_map/ppermute | solution.py:11
  128.7 3.9 %collective-permute-start.6 = (f32[128]{0:T(128)S(1)}, f32[128]{0:T(128)S(1)}, u32[]{:S(2)}, u32[]{:S(2)}) collective-permute-start(f32[128]{0:T(128)S(1)} %collective-permute-done.5), channel_id=1, source_target_pairs={{0,4},{4,8},{8,12},{12,16},{16,20},{20,24},{24,28},{28,0},{1,5},{5... | collective-permute-start | bytes 1544 | tf_op jit(solution)/shard_map/ppermute | solution.py:11
Sparse Core Ops, SparseCore 0:
  90.1 77.0 reduce-scatter.2
  170.7 36.4 reduce-scatter.4
